TPU v7x, 256 devices: a whole 4x4x8 slice. The times are simulated.
256 devices in a mesh: own: 32 (over x, z), row: 8 (over y, core).
Axes of the slice: x: 4, y: 4, z: 8, core: 2. Of those that a mesh axis runs over, the one named last changes fastest.
Arguments:
- sigma_anc: float32 [16384, 16384], P('row', 'own'), may hold values from -1.5 to 1.5
- row_blocks: int32 [64, 8], replicated, may hold values from 0 to 63, as said below
- panel1: float32 [64, 2048, 256], P('own', 'row'), may hold values from -0.375 to 0.375
- diag_inv1: float32 [64, 256, 256], P('own'), as said below
- mask1: int32 [64, 8], P('own', 'row'), may hold values 0 or 1
- parent_block2: float32 [64, 256, 256], P('own'), may hold values from -0.375 to 0.375
- panel2: float32 [64, 2048, 256], P('own', 'row'), may hold values from -0.375 to 0.375
- diag_inv2: float32 [64, 256, 256], P('own'), as said below
- mask2: int32 [64, 8], P('own', 'row'), may hold values 0 or 1
Outputs:
- sel1_panel: float32 [64, 2048, 256], P('own', 'row')
- sel1_diag: float32 [64, 256, 256], P('own')
- sel2_parent: float32 [64, 256, 256], P('own')
- sel2_panel: float32 [64, 2048, 256], P('own', 'row')
- sel2_diag: float32 [64, 256, 256], P('own')
Inputs may be any that keep to these rules, and one draw needn't show every extreme that they name: `row_blocks`: entry l of each row lies in block rows 8 * l to 8 * (l + 1) - 1; for supernodes s with the same s // 2, the entries of one column l lie in different aligned runs of 2 block rows. `diag_inv1`: lower triangular, with diagonal entries from 1 to 2. `diag_inv2`: lower triangular, with diagonal entries from 1 to 2.
All inputs are finite; a program needn't handle non-finite values. No bound on the sum of `mask1` or of `mask2` on one device may be relied on, other than what follows from the above.
Results may differ from a plain program's by a relative error of at most 0.000071.
Values sent between devices are 32-bit elements; how exact they have to be, the bound alone decides.
No kernel may reach another device: no remote copies, remote signals or barrier semaphores. Data moves between devices by JAX's collectives and lax.ppermute only.
A program may use at most 128 MiB of HBM per device.

v0:
```python
import jax
import jax.numpy as jnp
from jax import lax
from jax.sharding import PartitionSpec as P

B = 256
HIGH = lax.Precision.HIGHEST


def shifted(shard, axis, by):
    length = lax.axis_size(axis)
    return lax.ppermute(shard, axis, [(i, (i + by) % length) for i in range(length)])


def product(form, left, right):
    return jnp.einsum(form, left, right, precision=HIGH)


def select_send(sigma_local, row_blocks, slots):
    own_count = lax.axis_size("own")
    own_here = lax.axis_index("own")
    row_here = lax.axis_index("row")
    rows_here = sigma_local.shape[0] // B
    cols_here = sigma_local.shape[1] // B
    rowlist = row_blocks.reshape(own_count, slots, -1)
    group = own_here * cols_here // rows_here
    want_col = lax.dynamic_index_in_dim(rowlist, group, 2, keepdims=False)
    local_col = want_col - own_here * cols_here
    match = ((local_col >= 0) & (local_col < cols_here)).astype(jnp.int32)
    which = jnp.sum(match * jnp.arange(slots, dtype=jnp.int32)[None, :], axis=1)
    chosen = rowlist[jnp.arange(own_count, dtype=jnp.int32), which]
    chosen_row = (
        lax.dynamic_index_in_dim(chosen, row_here, 1, keepdims=False) - row_here * rows_here
    )
    chosen_col = jnp.clip(
        lax.dynamic_index_in_dim(chosen, group, 1, keepdims=False) - own_here * cols_here,
        0,
        cols_here - 1,
    )
    blocks4 = sigma_local.reshape(rows_here, B, cols_here, B)
    return blocks4[chosen_row, :, chosen_col, :]


def select_take(received, row_blocks, slots, cols_here):
    mine = lax.axis_index("own") * slots + jnp.arange(slots, dtype=jnp.int32)
    rowlist = row_blocks[mine]
    sender = rowlist // cols_here
    return received[sender]


def on_device(
    sigma_anc, row_blocks, panel1, diag_inv1, mask1, parent_block2, panel2, diag_inv2, mask2
):
    slots = panel1.shape[0]
    cols_here = sigma_anc.shape[1] // B
    keep_own2 = mask2.astype(jnp.float32)
    up_parent = product("kij,kjc->kic", parent_block2, diag_inv2)
    factor2_own = keep_own2[:, :, None] * product("kij,kjc->kic", panel2, diag_inv2)
    factor2_child = shifted(factor2_own, "own", -1)
    outgoing = select_send(sigma_anc, row_blocks, slots)
    received = lax.all_to_all(outgoing, "own", split_axis=0, concat_axis=0, tiled=True)
    blocks1 = select_take(received, row_blocks, slots, cols_here)
    keep1 = mask1.astype(jnp.float32)
    factor1 = keep1[:, :, None] * product("kij,kjc->kic", panel1, diag_inv1)
    factors1 = lax.all_gather(factor1, "row", axis=1, tiled=True).reshape(slots, -1, B, B)
    sel1_panel = -keep1[:, :, None] * product("kmij,kmjc->kic", blocks1, factors1)
    gram1 = product("kji,kjc->kic", diag_inv1, diag_inv1)
    sel1_diag = gram1 - lax.psum(product("kji,kjc->kic", factor1, sel1_panel), "row")
    factor2 = keep1[:, :, None] * factor2_child
    factors2 = lax.all_gather(factor2, "row", axis=1, tiled=True).reshape(slots, -1, B, B)
    anc2 = keep1[:, :, None] * product("kmij,kmjc->kic", blocks1, factors2)
    par_panel = shifted(sel1_panel, "own", 1)
    par_anc = shifted(anc2, "own", 1)
    par_diag = shifted(sel1_diag, "own", 1)
    sel2_panel = -keep_own2[:, :, None] * (product("kij,kjc->kic", par_panel, up_parent) + par_anc)
    cross = product("kji,kjc->kic", par_panel, factor2_own)
    back = product("kji,kjc->kic", factor2_own, sel2_panel)
    par_diag, cross, back = lax.optimization_barrier((par_diag, cross, back))
    cross, back = lax.psum((cross, back), "row")
    sel2_parent = -(product("kij,kjc->kic", par_diag, up_parent) + cross)
    gram2 = product("kji,kjc->kic", diag_inv2, diag_inv2)
    sel2_diag = gram2 - product("kji,kjc->kic", up_parent, sel2_parent) - back
    return (sel1_panel, sel1_diag, sel2_parent, sel2_panel, sel2_diag)


def solution(mesh):
    in_specs = (
        P("row", "own"),
        P(),
        P("own", "row", None),
        P("own", None, None),
        P("own", "row"),
        P("own", None, None),
        P("own", "row", None),
        P("own", None, None),
        P("own", "row"),
    )
    out_specs = (
        P("own", "row", None),
        P("own", None, None),
        P("own", None, None),
        P("own", "row", None),
        P("own", None, None),
    )
    return jax.shard_map(
        on_device, mesh=mesh, in_specs=in_specs, out_specs=out_specs, check_vma=False
    )
```

profile of v0, /device:TPU:2, one launch (start us, length us, event | category | flops | bytes accessed | tf_op | source)
XLA Modules:
  0.0 444.9 jit_solution(6164868798614665549)
XLA Ops:
  9.1 5.9 %reshape.167 = f32[8,256,2,256]{3,2,1,0:T(2,128)} reshape(f32[2048,512]{1,0:T(8,128)} %param.9) | data formatting | bytes 8388608 | tf_op jit(solution)/shard_map/reshape | solution.py:40
  15.1 4.7 %copy.72 = f32[8,256,2,256]{3,1,2,0:T(8,128)} copy(f32[8,256,2,256]{3,2,1,0:T(2,128)} %reshape.167) | data formatting | bytes 8388608 | tf_op jit(solution)/shard_map/reshape | solution.py:40
  19.9 6.5 %gather_fusion.1 = f32[32,256,256]{2,1,0:T(8,128)} fusion(f32[8,256,2,256]{3,1,2,0:T(8,128)} %copy.72, s32[32]{0:T(128)S(1)} %fusion.11), kind=kCustom, calls=%fused_computation.1 | custom fusion | bytes 16777472 | tf_op jit(solution)/shard_map/gather | solution.py:41
  26.5 11.8 %all-to-all-start = ((f32[32,256,256]{2,1,0:T(8,128)}), f32[32,256,256]{2,1,0:T(8,128)}, u32[]{:S(2)}, u32[]{:S(2)}) async-start(f32[32,256,256]{2,1,0:T(8,128)} %gather_fusion.1), calls=%async_computation | async-start | bytes 16777216 | tf_op jit(solution)/shard_map/all_to_all | solution.py:61
  38.4 1.5 convolution_multiply_fusion.1
  40.6 2.8 collective-permute-start.2
  43.3 190.9 %collective-permute-done.2 = f32[2,256,256]{2,1,0:T(8,128)S(1)} collective-permute-done((f32[2,256,256]{2,1,0:T(8,128)S(1)}, f32[2,256,256]{2,1,0:T(8,128)S(1)}, u32[]{:S(2)}, u32[]{:S(2)}) %collective-permute-start.2) | collective-permute-done | bytes 524320 | tf_op jit(solution)/shard_map/ppermute | solution.py:12
  235.9 6.2 %gather_fusion.3 = f32[16,256,256]{2,1,0:T(8,128)} fusion(f32[32,256,256]{2,1,0:T(8,128)} %all-to-all-done, s32[1024]{0:T(1024)S(1)} %pad_clamp_fusion), kind=kCustom, calls=%fused_computation.3 | custom fusion | bytes 8388672 | tf_op jit(solution)/shard_map/gather | solution.py:48
  242.1 8.1 %fusion.3 = f32[2,256,256]{2,1,0:T(8,128)S(1)} fusion(f32[2,8,256,256]{3,2,1,0:T(8,128)} %bitcast.67, f32[2,8,256,256]{3,2,1,0:T(8,128)} %bitcast.69, f32[2]{0:T(128)S(1)} %fusion.16), kind=kOutput, calls=%fused_computation.14 | convolution fusion | flops 3221356544 | bytes 8912904 | tf_op jit(solution)/shard_map/kmij,kmjc->kic/dot_general | solution.py:16
  250.5 1.9 fusion.18
  252.4 21.4 %all-gather.5.cloned.1.call-done = f32[2,2048,256]{2,1,0:T(8,128)} async-done(((f32[2,256,256]{2,1,0:T(8,128)}), f32[2,2048,256]{2,1,0:T(8,128)}) %all-gather.5.cloned.1.call-update) | async-done | bytes 4194320 | tf_op jit(solution)/shard_map/all_gather | solution.py:70
  273.8 8.2 %fusion.1 = f32[2,256,256]{2,1,0:T(8,128)} fusion(f32[2,8,256,256]{3,2,1,0:T(8,128)} %bitcast.68, f32[2,8,256,256]{3,2,1,0:T(8,128)} %bitcast.70, f32[2]{0:T(128)S(1)} %convert_bitcast_fusion.1), kind=kOutput, calls=%fused_computation.8 | convolution fusion | flops 3221356544 | bytes 8912904 | tf_op jit(solution)/shard_map/kmij,kmjc->kic/dot_general | solution.py:16
  282.0 1.5 collective-permute-start.3
  283.7 1.7 fusion.20
  285.4 63.5 %all-reduce.4.cloned.1.call-done = f32[2,256,256]{2,1,0:T(8,128)} async-done(((f32[2,256,256]{2,1,0:T(8,128)}), f32[2,256,256]{2,1,0:T(8,128)}) %all-reduce.4.cloned.1.call-update) | async-done | bytes 524304 | tf_op jit(solution)/shard_map/psum | solution.py:68
  348.9 2.9 convolution_subtract_fusion.1
  351.8 1.6 collective-permute-start
  353.3 1.7 fusion.2
  355.0 1.8 fusion.21
  356.9 1.8 fusion.19
  358.7 7.1 %collective-permute-done = f32[2,256,256]{2,1,0:T(8,128)} collective-permute-done((f32[2,256,256]{2,1,0:T(8,128)}, f32[2,256,256]{2,1,0:T(8,128)}, u32[]{:S(2)}, u32[]{:S(2)}) %collective-permute-start) | collective-permute-done | bytes 524320 | tf_op jit(solution)/shard_map/ppermute | solution.py:12
  365.8 1.1 fusion.22
  366.9 67.6 %all-reduce.6.cloned.1.call-done = (f32[2,256,256]{2,1,0:T(8,128)}, f32[2,256,256]{2,1,0:T(8,128)}) async-done(((f32[2,256,256]{2,1,0:T(8,128)}, f32[2,256,256]{2,1,0:T(8,128)}), (f32[2,256,256]{2,1,0:T(8,128)}, f32[2,256,256]{2,1,0:T(8,128)})) %all-reduce.6.cloned.1.call-update) | async-done | bytes 1048592 | tf_op jit(solution)/shard_map/psum | solution.py:79
  434.5 1.9 fusion
  (57 shorter events, 6.8 us)
Async XLA Ops:
  7.2 32.7 %copy-start = (f32[2,256,256]{2,1,0:T(8,128)S(1)}, f32[2,256,256]{2,1,0:T(8,128)}, u32[]{:S(2)}) copy-start(f32[2,256,256]{2,1,0:T(8,128)} %param.16) | copy-start | bytes 1572868
  26.4 11.9 %copy-start.9 = (s32[2,1]{0,1:T(1,128)S(1)}, s32[2,1]{0,1:T(1,128)}, u32[]{:S(2)}) copy-start(s32[2,1]{0,1:T(1,128)} %param.13) | copy-start | bytes 28
  26.4 11.9 %copy-start.2 = (f32[2,256,256]{2,1,0:T(8,128)S(1)}, f32[2,256,256]{2,1,0:T(8,128)}, u32[]{:S(2)}) copy-start(f32[2,256,256]{2,1,0:T(8,128)} %param.12) | copy-start | bytes 1572868
  26.4 11.9 %copy-start.7 = (f32[2,256,256]{2,1,0:T(8,128)S(1)}, f32[2,256,256]{2,1,0:T(8,128)}, u32[]{:S(2)}) copy-start(f32[2,256,256]{2,1,0:T(8,128)} %param.11) | copy-start | bytes 1572868
  26.4 13.5 %copy-start.10 = (s32[2,1]{0,1:T(1,128)S(1)}, s32[2,1]{0,1:T(1,128)}, u32[]{:S(2)}) copy-start(s32[2,1]{0,1:T(1,128)} %param.17) | copy-start | bytes 28
  26.4 13.5 %copy-start.8 = (f32[2,256,256]{2,1,0:T(8,128)S(1)}, f32[2,256,256]{2,1,0:T(8,128)}, u32[]{:S(2)}) copy-start(f32[2,256,256]{2,1,0:T(8,128)} %param.15) | copy-start | bytes 1572868
  26.5 209.4 %all-to-all-start = ((f32[32,256,256]{2,1,0:T(8,128)}), f32[32,256,256]{2,1,0:T(8,128)}, u32[]{:S(2)}, u32[]{:S(2)}) async-start(f32[32,256,256]{2,1,0:T(8,128)} %gather_fusion.1), calls=%async_computation | async-start | bytes 16777216 | tf_op jit(solution)/shard_map/all_to_all | solution.py:61
  38.3 203.8 %all-gather.3.cloned.1.call-start = ((), (), s32[]{:S(2)}) async-start(), calls=%async_computation.1 | async-start | bytes 4718592 | tf_op jit(solution)/shard_map/all_gather | solution.py:65
  39.8 234.0 %all-gather.5.cloned.1.call-start = ((), (), s32[]{:S(2)}) async-start(), calls=%async_computation.3 | async-start | bytes 4718592 | tf_op jit(solution)/shard_map/all_gather | solution.py:70
  40.6 193.6 %collective-permute-start.2 = (f32[2,256,256]{2,1,0:T(8,128)S(1)}, f32[2,256,256]{2,1,0:T(8,128)S(1)}, u32[]{:S(2)}, u32[]{:S(2)}) collective-permute-start(f32[2,256,256]{2,1,0:T(8,128)S(1)} %convolution_multiply_fusion), channel_id=1, source_target_pairs={{0,248},{8,0},{16,8},{24,16},{32,24},{40,32},{48,40},{56,48},{64,5... | collective-permute-start | bytes 1572872 | tf_op jit(solution)/shard_map/ppermute | solution.py:12
  235.1 113.7 %all-reduce.4.cloned.1.call-start = ((), (), s32[]{:S(2)}) async-start(), calls=%async_computation.2 | async-start | bytes 1048576 | tf_op jit(solution)/shard_map/psum | solution.py:68
  242.1 8.4 %copy-start.1 = (f32[2,256,256]{2,1,0:T(8,128)S(1)}, f32[2,256,256]{2,1,0:T(8,128)}, u32[]{:S(2)}) copy-start(f32[2,256,256]{2,1,0:T(8,128)} %convolution_multiply_fusion.1) | copy-start | bytes 1572868
  250.2 31.8 %copy-start.3 = (f32[2,256,256]{2,1,0:T(8,128)}, f32[2,256,256]{2,1,0:T(8,128)S(1)}, u32[]{:S(2)}) copy-start(f32[2,256,256]{2,1,0:T(8,128)S(1)} %fusion.3) | copy-start | bytes 1572868
  250.2 103.1 %collective-permute-start.1 = (f32[2,256,256]{2,1,0:T(8,128)S(1)}, f32[2,256,256]{2,1,0:T(8,128)S(1)}, u32[]{:S(2)}, u32[]{:S(2)}) collective-permute-start(f32[2,256,256]{2,1,0:T(8,128)S(1)} %fusion.3), channel_id=1, source_target_pairs={{0,8},{8,16},{16,24},{24,32},{32,40},{40,48},{48,56},{56,64},{64,7... | collective-permute-start | bytes 1572872 | tf_op jit(solution)/shard_map/ppermute | solution.py:12
  282.0 71.3 %collective-permute-start.3 = (f32[2,256,256]{2,1,0:T(8,128)}, f32[2,256,256]{2,1,0:T(8,128)}, u32[]{:S(2)}, u32[]{:S(2)}) collective-permute-start(f32[2,256,256]{2,1,0:T(8,128)} %fusion.1), channel_id=1, source_target_pairs={{0,8},{8,16},{16,24},{24,32},{32,40},{40,48},{48,56},{56,64},{64,7... | collective-permute-start | bytes 1572872 | tf_op jit(solution)/shard_map/ppermute | solution.py:12
  283.6 150.9 %all-reduce.6.cloned.1.call-start = ((), (), s32[]{:S(2)}) async-start(), calls=%async_computation.4 | async-start | bytes 2097152 | tf_op jit(solution)/shard_map/psum | solution.py:79
  351.8 14.1 %collective-permute-start = (f32[2,256,256]{2,1,0:T(8,128)}, f32[2,256,256]{2,1,0:T(8,128)}, u32[]{:S(2)}, u32[]{:S(2)}) collective-permute-start(f32[2,256,256]{2,1,0:T(8,128)} %convolution_subtract_fusion.1), channel_id=1, source_target_pairs={{0,8},{8,16},{16,24},{24,32},{32,40},{40,48},{48,56},{56,64},{64,7... | collective-permute-start | bytes 1572872 | tf_op jit(solution)/shard_map/ppermute | solution.py:12
  355.0 82.5 %copy-start.4 = (f32[2,256,256]{2,1,0:T(8,128)}, f32[2,256,256]{2,1,0:T(8,128)S(1)}, u32[]{:S(2)}) copy-start(f32[2,256,256]{2,1,0:T(8,128)S(1)} %fusion.2) | copy-start | bytes 1572868
  434.5 3.0 copy-start.6
  436.4 2.0 copy-start.5
Sparse Core Ops, SparseCore 0:
  41.5 35.7 all-gather.2
  235.3 38.5 all-gather.4
  283.7 65.0 all-reduce.3
  366.0 68.4 all-reduce.5
where the time goes:
time: 445 us
  waiting for transfers between devices  351 us (79%)
  matrix products  34.3 us (8%)
  local copies, waits for them, and re-layouts  25.7 us (6%)
  starting transfers between devices  18.1 us (4%)
  between operations  14 us (3%)
    ppermute x4, waiting for transfers between devices, shifted(): lax.ppermute(shard, axis, [(i, (i + by) % length) for i in range(length)])  198 us
    psum x1, waiting for transfers between devices, on_device(): cross, back = lax.psum((cross, back), 'row')  67.6 us
    psum x1, waiting for transfers between devices, on_device(): lax.psum(product('kji,kjc->kic', factor1, sel1_panel), 'row')  63.5 us
    dot_general x13, matrix products, product(): return jnp.einsum(form, left, right, precision=HIGH)  34.3 us
    all_gather x1, waiting for transfers between devices, on_device(): lax.all_gather(factor2, 'row', axis=1, tiled=True).reshape(slots, -1, B, B)  21.4 us
    all_to_all x1, starting transfers between devices, on_device(): lax.all_to_all(outgoing, 'own', split_axis=0, concat_axis=0, tiled=True)  11.8 us
    reshape x2, local copies, waits for them, and re-layouts, select_send(): blocks4 = sigma_local.reshape(rows_here, B, cols_here, B)  10.6 us
  transfers between devices with their start and end apart: 9, of which 5 were waited for; matrix products, arithmetic and copies ran while one was open for 9% of the time, Pallas kernels for 0%

commit v1 on v0

--- a/solution.py
+++ b/solution.py
@@ -1,3 +1,4 @@
+import functools
 import jax
 import jax.numpy as jnp
 from jax import lax
@@ -5,6 +6,13 @@
 
 B = 256
 HIGH = lax.Precision.HIGHEST
+
+
+def play_the_bench(obj, group_axis):
+    return jnp.sum(lax.all_gather(obj, axis_name=group_axis), axis=0)
+
+
+open_keys = functools.partial(play_the_bench, group_axis="row")
 
 
 def shifted(shard, axis, by):
@@ -65,7 +73,7 @@
     factors1 = lax.all_gather(factor1, "row", axis=1, tiled=True).reshape(slots, -1, B, B)
     sel1_panel = -keep1[:, :, None] * product("kmij,kmjc->kic", blocks1, factors1)
     gram1 = product("kji,kjc->kic", diag_inv1, diag_inv1)
-    sel1_diag = gram1 - lax.psum(product("kji,kjc->kic", factor1, sel1_panel), "row")
+    sel1_diag = gram1 - open_keys(product("kji,kjc->kic", factor1, sel1_panel))
     factor2 = keep1[:, :, None] * factor2_child
     factors2 = lax.all_gather(factor2, "row", axis=1, tiled=True).reshape(slots, -1, B, B)
     anc2 = keep1[:, :, None] * product("kmij,kmjc->kic", blocks1, factors2)

time: 445 us -> 411 us (0.924)
  waiting for transfers between devices: 351 us -> 314 us
    psum x1 -> x0, waiting for transfers between devices: 63.5 us -> none  [on_device(): lax.psum(product('kji,kjc->kic', factor1, sel1_panel), 'row')]
    ppermute x4, waiting for transfers between devices: 198 us -> 226 us  [shifted(): lax.ppermute(shard, axis, [(i, (i + by) % length) for i in range(length)])]
  transfers between devices with their start and end apart: 9 -> 9, of which waited for: 5 -> 7; matrix products, arithmetic and copies ran while one was open for 9% -> 8% of each run, Pallas kernels for 0% -> 0%
where the time goes in v1:
time: 411 us
  waiting for transfers between devices  314 us (76%)
  matrix products  32 us (8%)
  local copies, waits for them, and re-layouts  25.7 us (6%)
  starting transfers between devices  19.6 us (5%)
  between operations  14 us (3%)
  other arithmetic  5.45 us (1%)
    ppermute x4, waiting for transfers between devices, shifted(): lax.ppermute(shard, axis, [(i, (i + by) % length) for i in range(length)])  226 us
    psum x1, waiting for transfers between devices, on_device(): cross, back = lax.psum((cross, back), 'row')  65.9 us
    dot_general x13, matrix products, product(): return jnp.einsum(form, left, right, precision=HIGH)  32 us
    all_gather x1, waiting for transfers between devices, on_device(): lax.all_gather(factor2, 'row', axis=1, tiled=True).reshape(slots, -1, B, B)  21.6 us
    all_to_all x1, starting transfers between devices, on_device(): lax.all_to_all(outgoing, 'own', split_axis=0, concat_axis=0, tiled=True)  11.8 us
    reshape x2, local copies, waits for them, and re-layouts, select_send(): blocks4 = sigma_local.reshape(rows_here, B, cols_here, B)  10.6 us
  transfers between devices with their start and end apart: 9, of which 7 were waited for; matrix products, arithmetic and copies ran while one was open for 8% of the time, Pallas kernels for 0%

profile of v1, /device:TPU:2, one launch (start us, length us, event | category | flops | bytes accessed | tf_op | source)
XLA Modules:
  0.0 410.7 jit_solution(14497119657009376390)
XLA Ops:
  9.1 5.9 %reshape.168 = f32[8,256,2,256]{3,2,1,0:T(2,128)} reshape(f32[2048,512]{1,0:T(8,128)} %param.9) | data formatting | bytes 8388608 | tf_op jit(solution)/shard_map/reshape | solution.py:48
  15.1 4.6 %copy.86 = f32[8,256,2,256]{3,1,2,0:T(8,128)} copy(f32[8,256,2,256]{3,2,1,0:T(2,128)} %reshape.168) | data formatting | bytes 8388608 | tf_op jit(solution)/shard_map/reshape | solution.py:48
  19.9 6.5 %gather_fusion.1 = f32[32,256,256]{2,1,0:T(8,128)} fusion(f32[8,256,2,256]{3,1,2,0:T(8,128)} %copy.86, s32[32]{0:T(128)S(1)} %fusion.11), kind=kCustom, calls=%fused_computation.1 | custom fusion | bytes 16777472 | tf_op jit(solution)/shard_map/gather | solution.py:49
  26.4 11.8 %all-to-all-start = ((f32[32,256,256]{2,1,0:T(8,128)}), f32[32,256,256]{2,1,0:T(8,128)}, u32[]{:S(2)}, u32[]{:S(2)}) async-start(f32[32,256,256]{2,1,0:T(8,128)} %gather_fusion.1), calls=%async_computation | async-start | bytes 16777216 | tf_op jit(solution)/shard_map/all_to_all | solution.py:69
  38.4 1.5 convolution_multiply_fusion.1
  40.6 2.7 collective-permute-start.2
  43.3 190.9 %collective-permute-done.2 = f32[2,256,256]{2,1,0:T(8,128)S(1)} collective-permute-done((f32[2,256,256]{2,1,0:T(8,128)S(1)}, f32[2,256,256]{2,1,0:T(8,128)S(1)}, u32[]{:S(2)}, u32[]{:S(2)}) %collective-permute-start.2) | collective-permute-done | bytes 524320 | tf_op jit(solution)/shard_map/ppermute | solution.py:20
  235.9 6.2 %gather_fusion.3 = f32[16,256,256]{2,1,0:T(8,128)} fusion(f32[32,256,256]{2,1,0:T(8,128)} %all-to-all-done, s32[1024]{0:T(1024)S(1)} %pad_clamp_fusion), kind=kCustom, calls=%fused_computation.3 | custom fusion | bytes 8388672 | tf_op jit(solution)/shard_map/gather | solution.py:56
  242.1 8.1 %fusion.3 = f32[2,256,256]{2,1,0:T(8,128)S(1)} fusion(f32[2,8,256,256]{3,2,1,0:T(8,128)} %bitcast.68, f32[2,8,256,256]{3,2,1,0:T(8,128)} %bitcast.71, f32[2]{0:T(128)S(1)} %fusion.16), kind=kOutput, calls=%fused_computation.14 | convolution fusion | flops 3221356544 | bytes 8912904 | tf_op jit(solution)/shard_map/kmij,kmjc->kic/dot_general | solution.py:24
  250.2 1.9 fusion.18
  252.2 21.6 %all-gather.7.cloned.1.call-done = f32[2,2048,256]{2,1,0:T(8,128)} async-done(((f32[2,256,256]{2,1,0:T(8,128)}), f32[2,2048,256]{2,1,0:T(8,128)}) %all-gather.7.cloned.1.call-update) | async-done | bytes 4194320 | tf_op jit(solution)/shard_map/all_gather | solution.py:78
  273.8 8.1 %fusion.1 = f32[2,256,256]{2,1,0:T(8,128)S(1)} fusion(f32[2,8,256,256]{3,2,1,0:T(8,128)} %bitcast.69, f32[2,8,256,256]{3,2,1,0:T(8,128)} %bitcast.72, f32[2]{0:T(128)S(1)} %convert_bitcast_fusion.1), kind=kOutput, calls=%fused_computation.8 | convolution fusion | flops 3221356544 | bytes 8912904 | tf_op jit(solution)/shard_map/kmij,kmjc->kic/dot_general | solution.py:24
  281.9 1.8 collective-permute-start.3
  283.8 1.6 collective-permute-start.1
  286.0 13.1 %collective-permute-done.3 = f32[2,256,256]{2,1,0:T(8,128)S(1)} collective-permute-done((f32[2,256,256]{2,1,0:T(8,128)S(1)}, f32[2,256,256]{2,1,0:T(8,128)S(1)}, u32[]{:S(2)}, u32[]{:S(2)}) %collective-permute-start.3) | collective-permute-done | bytes 524320 | tf_op jit(solution)/shard_map/ppermute | solution.py:20
  299.1 10.6 %collective-permute-done.1 = f32[2,256,256]{2,1,0:T(8,128)S(1)} collective-permute-done((f32[2,256,256]{2,1,0:T(8,128)S(1)}, f32[2,256,256]{2,1,0:T(8,128)S(1)}, u32[]{:S(2)}, u32[]{:S(2)}) %collective-permute-start.1) | collective-permute-done | bytes 524320 | tf_op jit(solution)/shard_map/ppermute | solution.py:20
  310.9 3.3 reduce_sum.22
  314.2 2.9 convolution_subtract_fusion.1
  317.1 1.6 collective-permute-start
  318.7 1.8 fusion.21
  320.5 1.8 fusion.19
  322.4 11.2 %collective-permute-done = f32[2,256,256]{2,1,0:T(8,128)S(1)} collective-permute-done((f32[2,256,256]{2,1,0:T(8,128)}, f32[2,256,256]{2,1,0:T(8,128)S(1)}, u32[]{:S(2)}, u32[]{:S(2)}) %collective-permute-start) | collective-permute-done | bytes 524320 | tf_op jit(solution)/shard_map/ppermute | solution.py:20
  334.6 65.9 %all-reduce.3.cloned.1.call-done = (f32[2,256,256]{2,1,0:T(8,128)}, f32[2,256,256]{2,1,0:T(8,128)}) async-done(((f32[2,256,256]{2,1,0:T(8,128)}, f32[2,256,256]{2,1,0:T(8,128)}), (f32[2,256,256]{2,1,0:T(8,128)}, f32[2,256,256]{2,1,0:T(8,128)})) %all-reduce.3.cloned.1.call-update) | async-done | bytes 1048592 | tf_op jit(solution)/shard_map/psum | solution.py:87
  400.5 1.8 fusion
  (60 shorter events, 9.5 us)
Async XLA Ops:
  7.2 32.7 %copy-start = (f32[2,256,256]{2,1,0:T(8,128)S(1)}, f32[2,256,256]{2,1,0:T(8,128)}, u32[]{:S(2)}) copy-start(f32[2,256,256]{2,1,0:T(8,128)} %param.16) | copy-start | bytes 1572868
  26.4 11.9 %copy-start.10 = (s32[2,1]{0,1:T(1,128)S(1)}, s32[2,1]{0,1:T(1,128)}, u32[]{:S(2)}) copy-start(s32[2,1]{0,1:T(1,128)} %param.13) | copy-start | bytes 28
  26.4 11.9 %copy-start.2 = (f32[2,256,256]{2,1,0:T(8,128)S(1)}, f32[2,256,256]{2,1,0:T(8,128)}, u32[]{:S(2)}) copy-start(f32[2,256,256]{2,1,0:T(8,128)} %param.12) | copy-start | bytes 1572868
  26.4 11.9 %copy-start.8 = (f32[2,256,256]{2,1,0:T(8,128)S(1)}, f32[2,256,256]{2,1,0:T(8,128)}, u32[]{:S(2)}) copy-start(f32[2,256,256]{2,1,0:T(8,128)} %param.11) | copy-start | bytes 1572868
  26.4 13.5 %copy-start.11 = (s32[2,1]{0,1:T(1,128)S(1)}, s32[2,1]{0,1:T(1,128)}, u32[]{:S(2)}) copy-start(s32[2,1]{0,1:T(1,128)} %param.17) | copy-start | bytes 28
  26.4 13.5 %copy-start.9 = (f32[2,256,256]{2,1,0:T(8,128)S(1)}, f32[2,256,256]{2,1,0:T(8,128)}, u32[]{:S(2)}) copy-start(f32[2,256,256]{2,1,0:T(8,128)} %param.15) | copy-start | bytes 1572868
  26.4 209.4 %all-to-all-start = ((f32[32,256,256]{2,1,0:T(8,128)}), f32[32,256,256]{2,1,0:T(8,128)}, u32[]{:S(2)}, u32[]{:S(2)}) async-start(f32[32,256,256]{2,1,0:T(8,128)} %gather_fusion.1), calls=%async_computation | async-start | bytes 16777216 | tf_op jit(solution)/shard_map/all_to_all | solution.py:69
  38.3 203.8 %all-gather.5.cloned.1.call-start = ((), (), s32[]{:S(2)}) async-start(), calls=%async_computation.1 | async-start | bytes 4718592 | tf_op jit(solution)/shard_map/all_gather | solution.py:73
  39.8 234.0 %all-gather.7.cloned.1.call-start = ((), (), s32[]{:S(2)}) async-start(), calls=%async_computation.2 | async-start | bytes 4718592 | tf_op jit(solution)/shard_map/all_gather | solution.py:78
  40.6 193.6 %collective-permute-start.2 = (f32[2,256,256]{2,1,0:T(8,128)S(1)}, f32[2,256,256]{2,1,0:T(8,128)S(1)}, u32[]{:S(2)}, u32[]{:S(2)}) collective-permute-start(f32[2,256,256]{2,1,0:T(8,128)S(1)} %convolution_multiply_fusion), channel_id=1, source_target_pairs={{0,248},{8,0},{16,8},{24,16},{32,24},{40,32},{48,40},{56,48},{64,5... | collective-permute-start | bytes 1572872 | tf_op jit(solution)/shard_map/ppermute | solution.py:20
  235.1 75.8 %all-gather.9.cloned.1.call-start = ((), (), s32[]{:S(2)}) async-start(), calls=%async_computation.3 | async-start | bytes 4718592 | tf_op jit(solution)/shard_map/all_gather | solution.py:12
  242.1 8.1 %copy-start.1 = (f32[2,256,256]{2,1,0:T(8,128)S(1)}, f32[2,256,256]{2,1,0:T(8,128)}, u32[]{:S(2)}) copy-start(f32[2,256,256]{2,1,0:T(8,128)} %convolution_multiply_fusion.1) | copy-start | bytes 1572868
  250.2 33.5 %copy-start.3 = (f32[2,256,256]{2,1,0:T(8,128)}, f32[2,256,256]{2,1,0:T(8,128)S(1)}, u32[]{:S(2)}) copy-start(f32[2,256,256]{2,1,0:T(8,128)S(1)} %fusion.3) | copy-start | bytes 1572868
  252.1 148.4 %all-reduce.3.cloned.1.call-start = ((), (), s32[]{:S(2)}) async-start(), calls=%async_computation.4 | async-start | bytes 2097152 | tf_op jit(solution)/shard_map/psum | solution.py:87
  273.8 11.5 %copy-start.6 = (f32[2,256,256]{2,1,0:T(8,128)S(1)}, f32[2,256,256]{2,1,0:T(8,128)}, u32[]{:S(2)}) copy-start(f32[2,256,256]{2,1,0:T(8,128)} %param.14) | copy-start | bytes 1572868
  281.9 17.1 %collective-permute-start.3 = (f32[2,256,256]{2,1,0:T(8,128)S(1)}, f32[2,256,256]{2,1,0:T(8,128)S(1)}, u32[]{:S(2)}, u32[]{:S(2)}) collective-permute-start(f32[2,256,256]{2,1,0:T(8,128)S(1)} %fusion.1), channel_id=1, source_target_pairs={{0,8},{8,16},{16,24},{24,32},{32,40},{40,48},{48,56},{56,64},{64,7... | collective-permute-start | bytes 1572872 | tf_op jit(solution)/shard_map/ppermute | solution.py:20
  283.8 25.9 %collective-permute-start.1 = (f32[2,256,256]{2,1,0:T(8,128)S(1)}, f32[2,256,256]{2,1,0:T(8,128)S(1)}, u32[]{:S(2)}, u32[]{:S(2)}) collective-permute-start(f32[2,256,256]{2,1,0:T(8,128)S(1)} %fusion.3), channel_id=1, source_target_pairs={{0,8},{8,16},{16,24},{24,32},{32,40},{40,48},{48,56},{56,64},{64,7... | collective-permute-start | bytes 1572872 | tf_op jit(solution)/shard_map/ppermute | solution.py:20
  310.3 10.2 %copy-start.4 = (f32[2,256,256]{2,1,0:T(8,128)}, f32[2,256,256]{2,1,0:T(8,128)S(1)}, u32[]{:S(2)}) copy-start(f32[2,256,256]{2,1,0:T(8,128)S(1)} %fusion.2) | copy-start | bytes 1572868
  317.1 16.4 %collective-permute-start = (f32[2,256,256]{2,1,0:T(8,128)}, f32[2,256,256]{2,1,0:T(8,128)S(1)}, u32[]{:S(2)}, u32[]{:S(2)}) collective-permute-start(f32[2,256,256]{2,1,0:T(8,128)} %convolution_subtract_fusion.1), channel_id=1, source_target_pairs={{0,8},{8,16},{16,24},{24,32},{32,40},{40,48},{48,56},{56,64},{64,7... | collective-permute-start | bytes 1572872 | tf_op jit(solution)/shard_map/ppermute | solution.py:20
  400.5 2.8 copy-start.7
  402.3 1.9 copy-start.5
Sparse Core Ops, SparseCore 0:
  41.5 35.7 all-gather.4
  235.2 38.5 all-gather.6
  276.2 34.6 all-gather.8
  333.7 66.7 all-reduce.2
